TPU v7x, 256 devices: a whole 4x4x8 slice. The times are simulated.
256 devices in a mesh: seq: 8 (over x, core), vocab: 32 (over z, y).
Axes of the slice: x: 4, y: 4, z: 8, core: 2. Of those that a mesh axis runs over, the one named last changes fastest.
Arguments:
- hidden: bfloat16 [2048, 4096], P('seq'), may hold values from -48 to 48
- head_weight: bfloat16 [4096, 65536], P('seq', 'vocab'), may hold values from -0.09375 to 0.09375
- queries: float32 [16, 65536], P(None, 'vocab'), may hold values from 0 to 1, as said below
- passage_lengths: int32 [32], replicated, may hold values from 1 to 192, 2048 in all
- pairing: int32 [32], replicated, may hold values from 0 to 15
- doc_freq: int32 [65536], P('vocab'), may hold values from 0 to 4194304
Outputs:
- grad_hidden: bfloat16 [2048, 4096], P('seq', 'vocab')
- losses: float32 [2], replicated
Inputs may be any that keep to these rules, and one draw needn't show every extreme that they name: `queries`: entries are nonnegative.
All inputs are finite; a program needn't handle non-finite values.
Results may differ from a plain program's by a relative error of at most 0.0039.
Values may be sent and summed in bfloat16 or wider, within the bound.
No kernel may reach another device: no remote copies, remote signals or barrier semaphores. Data moves between devices by JAX's collectives and lax.ppermute only.
A program may use at most 128 MiB of HBM per device.

v0:
```python
import jax
import jax.numpy as jnp
from jax import lax
from jax.sharding import PartitionSpec as P

DOCS = 4194304
sharpness = 8.0
loss_scale = 16384.0
flops_weight = 32.0
highest = lax.Precision.HIGHEST


def softmax_terms(scores, pair_rows):
    onehot = (jnp.arange(scores.shape[0], dtype=jnp.int32)[:, None] == pair_rows[None, :]).astype(
        jnp.float32
    )
    peak_score = jnp.max(scores, axis=0)
    shifted = jnp.exp(scores - peak_score[None, :])
    denominator = jnp.sum(shifted, axis=0)
    log_total = peak_score + jnp.log(denominator)
    losses_each = log_total - jnp.sum(onehot * scores, axis=0)
    return (losses_each, shifted / denominator[None, :] - onehot)


def per_device(hidden, head_weight, queries, passage_lengths, pairing, doc_freq):
    tok_rows = hidden.shape[0]
    vocab_cols = head_weight.shape[1]
    passages = passage_lengths.shape[0]
    vocab_total = vocab_cols * lax.axis_size("vocab")
    finish = jnp.cumsum(passage_lengths)
    starts = finish - passage_lengths
    position = lax.axis_index("seq") * tok_rows + jnp.arange(tok_rows, dtype=jnp.int32)
    member = (
        (position[None, :] >= starts[:, None]) & (position[None, :] < finish[:, None])
    ).astype(jnp.float32)
    counts = passage_lengths.astype(jnp.float32)
    weights_df = jnp.log(1.0 + DOCS / (1.0 + doc_freq.astype(jnp.float32)))
    flops_grad = loss_scale * flops_weight * 2.0 / (vocab_total * passages)
    full_head = lax.all_gather(head_weight, "seq", axis=0, tiled=True)
    logits = jnp.dot(hidden, full_head, preferred_element_type=jnp.float32)
    lifted = 1.0 + jax.nn.relu(logits)
    squared = lifted * lifted
    fourth = squared * squared
    powered = fourth * fourth
    local_sums = jnp.dot(member, powered, precision=highest)
    totals = lax.psum(local_sums, "seq")
    pooled = (jnp.log(totals) - jnp.log(counts)[:, None]) / sharpness
    col_mean = jnp.sum(pooled, axis=0) / passages
    flops_part = jnp.sum(weights_df * col_mean * col_mean) / vocab_total
    scores, flops_value = lax.psum(
        (jnp.dot(queries, pooled.T, precision=highest), flops_part), "vocab"
    )
    losses_each, probs = softmax_terms(scores, pairing)
    contrast = jnp.mean(losses_each)
    dscores = probs * (loss_scale / passages)
    dpooled = jnp.dot(dscores.T, queries, precision=highest) + flops_grad * weights_df * col_mean
    factor = dpooled / totals
    spread = lax.dot_general(member, factor, (((0,), (0,)), ((), ())), precision=highest)
    seventh = fourth * squared * lifted
    dlogits = jnp.where(logits > 0, spread * seventh, 0.0).astype(jnp.bfloat16)
    grad_cols = lax.psum_scatter(
        lax.dot_general(
            full_head, dlogits, (((1,), (1,)), ((), ())), preferred_element_type=jnp.float32
        ),
        "vocab",
        scatter_dimension=0,
        tiled=True,
    )
    losses = jnp.stack([contrast, flops_value])
    return (grad_cols.T.astype(jnp.bfloat16), losses)


def solution(mesh):
    placed = (P("seq", None), P("seq", "vocab"), P(None, "vocab"), P(), P(), P("vocab"))
    return jax.shard_map(
        per_device, mesh=mesh, in_specs=placed, out_specs=(P("seq", "vocab"), P()), check_vma=False
    )
```

profile of v0, /device:TPU:2, one launch (start us, length us, event | category | flops | bytes accessed | tf_op | source)
XLA Modules:
  0.0 500.4 jit_solution(3179952712906589109)
XLA Ops:
  7.2 0.0 all-gather.2.cloned.1.call-start
  7.2 0.7 all-gather.2.cloned.1.call-update
  7.9 0.0 all-reduce.3.cloned.1.call-start
  8.0 0.1 copy.9
  8.1 0.1 reduce-window.8
  8.1 0.1 reduce
  8.3 91.6 %all-gather.2.cloned.1.call-done = bf16[4096,2048]{1,0:T(8,128)(2,1)} async-done(((bf16[512,2048]{1,0:T(8,128)(2,1)}), bf16[4096,2048]{1,0:T(8,128)(2,1)}) %all-gather.2.cloned.1.call-update) | async-done | bytes 16777232 | tf_op jit(solution)/shard_map/all_gather | solution.py:39
  99.9 8.1 %fusion.31 = f32[256,2048]{1,0:T(8,128)S(1)} fusion(bf16[256,4096]{1,0:T(8,128)(2,1)S(1)} %copy-done, bf16[4096,2048]{1,0:T(8,128)(2,1)} %all-gather.2.cloned.1.call-done), kind=kOutput, calls=%fused_computation.51 | convolution fusion | flops 4294967296 | bytes 20971520 | tf_op jit(solution)/shard_map/dot_general | solution.py:40
  108.0 1.3 copy-done.5
  109.4 1.9 fusion.3
  111.3 0.0 all-reduce.3.cloned.1.call-update
  111.3 0.0 reduce-scatter.2.cloned.1.call-start
  111.4 64.3 %all-reduce.3.cloned.1.call-done = f32[32,2048]{1,0:T(8,128)} async-done(((f32[32,2048]{1,0:T(8,128)}), f32[32,2048]{1,0:T(8,128)}) %all-reduce.3.cloned.1.call-update) | async-done | bytes 262160 | tf_op jit(solution)/shard_map/psum | solution.py:46
  175.6 1.1 fusion.8
  176.7 0.6 fusion.17
  178.0 1.3 convolution_bitcast_fusion.1
  179.3 78.1 %all-reduce = (f32[16,32]{1,0:T(8,128)S(1)}, f32[1]{0:T(128)}) all-reduce(f32[16,32]{1,0:T(8,128)S(1)} %convolution_bitcast_fusion.1, f32[1]{0:T(128)} %bitcast.5), channel_id=1, replica_groups=mesh['seq'=8,'vocab'=32] {'vocab'}, use_global_device_ids=true, to_apply=%region_2.3 | all-reduce | flops 513 | bytes 4104 | tf_op jit(solution)/shard_map/psum | solution.py:50
  257.5 1.4 fusion.2
  258.8 3.2 fusion.1
  262.0 10.1 %convolution_bitcast_fusion = f32[4096,256]{0,1:T(8,128)} fusion(bf16[256,2048]{1,0:T(8,128)(2,1)S(1)} %fusion.1, bf16[4096,2048]{1,0:T(8,128)(2,1)} %all-gather.2.cloned.1.call-done), kind=kOutput, calls=%fused_computation | convolution fusion | flops 4294967296 | bytes 22020096 | tf_op jit(solution)/shard_map/dot_general | solution.py:62
  272.1 0.6 subtract_reduce_fusion
  273.4 1.2 pad_maximum_fusion
  274.6 217.8 %reduce-scatter.2.cloned.1.call-done = f32[128,256]{0,1:T(8,128)} async-done(((f32[4096,256]{0,1:T(8,128)}), f32[128,256]{0,1:T(8,128)}) %reduce-scatter.2.cloned.1.call-update) | async-done | bytes 131088 | tf_op jit(solution)/shard_map/reduce_scatter | solution.py:61
  492.4 1.5 convert_bitcast_fusion
  (17 shorter events, 0.1 us)
Async XLA Ops:
  7.2 92.7 %copy-start = (bf16[256,4096]{1,0:T(8,128)(2,1)S(1)}, bf16[256,4096]{1,0:T(8,128)(2,1)}, u32[]{:S(2)}) copy-start(bf16[256,4096]{1,0:T(8,128)(2,1)} %param.6) | copy-start | bytes 6291460
  7.2 0.8 copy-start.3
  7.2 92.7 %all-gather.2.cloned.1.call-start = ((), (), s32[]{:S(2)}) async-start(), calls=%async_computation.1 | async-start | bytes 18874368 | tf_op jit(solution)/shard_map/all_gather | solution.py:39
  7.9 167.7 %all-reduce.3.cloned.1.call-start = ((), (), s32[]{:S(2)}) async-start(), calls=%async_computation.2 | async-start | bytes 524288 | tf_op jit(solution)/shard_map/psum | solution.py:46
  108.0 1.4 copy-start.5
  109.4 67.3 %copy-start.2 = (s32[2048]{0:T(1024)S(1)}, s32[2048]{0:T(1024)}, u32[]{:S(2)}) copy-start(s32[2048]{0:T(1024)} %param.11) | copy-start | bytes 24580
  109.4 68.6 %copy-start.1 = (f32[16,2048]{1,0:T(8,128)S(1)}, f32[16,2048]{1,0:T(8,128)}, u32[]{:S(2)}) copy-start(f32[16,2048]{1,0:T(8,128)} %param.8) | copy-start | bytes 393220
  109.4 148.1 %copy-start.4 = (s32[32]{0:T(128)S(1)}, s32[32]{0:T(128)}, u32[]{:S(2)}) copy-start(s32[32]{0:T(128)} %param.10) | copy-start | bytes 388
  111.3 381.1 %reduce-scatter.2.cloned.1.call-start = ((), (), s32[]{:S(2)}) async-start(), calls=%async_computation.3 | async-start | bytes 4325376 | tf_op jit(solution)/shard_map/reduce_scatter | solution.py:61
Sparse Core Ops, SparseCore 0:
  9.9 89.9 all-gather.1
  111.4 64.1 all-reduce.2
  272.3 220.0 reduce-scatter.1
where the time goes:
time: 501 us; the launch traced here: 500 us
  waiting for transfers between devices  374 us (75%)
  blocking collectives  78.1 us (16%)
  matrix products  25.9 us (5%)
  between operations  15.1 us (3%)
  other arithmetic  5.3 us (1%)
    reduce_scatter x1, waiting for transfers between devices, per_device(): lax.psum_scatter(lax.dot_general(full_head, dlogits, (((1,), (1,)), ((),...  218 us
    all_gather x1, waiting for transfers between devices, per_device(): full_head = lax.all_gather(head_weight, 'seq', axis=0, tiled=True)  91.6 us
    psum x1, blocking collectives, per_device(): lax.psum((jnp.dot(queries, pooled.T, precision=highest), flops_part), 'vo...  78.1 us
    psum x1, waiting for transfers between devices, per_device(): totals = lax.psum(local_sums, 'seq')  64.3 us
    dot_general x1, matrix products, per_device(): lax.dot_general(full_head, dlogits, (((1,), (1,)), ((), ())), preferred_e...  10.1 us
  transfers between devices with their start and end apart: 3, of which 3 were waited for; matrix products, arithmetic and copies ran while one was open for 0% of the time, Pallas kernels for 0%

commit v1 on v0

--- a/solution.py
+++ b/solution.py
@@ -36,7 +36,21 @@
     counts = passage_lengths.astype(jnp.float32)
     weights_df = jnp.log(1.0 + DOCS / (1.0 + doc_freq.astype(jnp.float32)))
     flops_grad = loss_scale * flops_weight * 2.0 / (vocab_total * passages)
-    full_head = lax.all_gather(head_weight, "seq", axis=0, tiled=True)
+    ways, here, turn = (lax.axis_size("seq"), lax.axis_index("seq"), head_weight.shape[0])
+    dims = [n * ways if d == 0 else n for d, n in enumerate(head_weight.shape)]
+    full = lax.dynamic_update_slice_in_dim(
+        jnp.zeros(dims, head_weight.dtype), head_weight, here * turn, axis=0
+    )
+    going_up = going_down = head_weight
+    for far in range(1, ways // 2 + 1):
+        going_up = lax.ppermute(going_up, "seq", [(d, (d + 1) % ways) for d in range(ways)])
+        full = lax.dynamic_update_slice_in_dim(full, going_up, (here - far) % ways * turn, axis=0)
+        if 2 * far < ways:
+            going_down = lax.ppermute(going_down, "seq", [(d, (d - 1) % ways) for d in range(ways)])
+            full = lax.dynamic_update_slice_in_dim(
+                full, going_down, (here + far) % ways * turn, axis=0
+            )
+    full_head = full
     logits = jnp.dot(hidden, full_head, preferred_element_type=jnp.float32)
     lifted = 1.0 + jax.nn.relu(logits)
     squared = lifted * lifted

time: 501 us -> 516 us (1.030)
  local copies, waits for them, and re-layouts: 1.46 us -> 20.7 us
  waiting for transfers between devices: 374 us -> 368 us
    all_gather x1 -> x0, waiting for transfers between devices: 91.6 us -> none  [per_device(): full_head = lax.all_gather(head_weight, 'seq', axis=0, tiled=True)]
    ppermute x0 -> x7, waiting for transfers between devices: none -> 82.6 us  [the longest x4 82.6 us: per_device(): lax.ppermute(going_up, 'seq', [(d, (d + 1) % ways) for d in range(ways)])]
    dynamic_update_slice x0 -> x8, local copies, waits for them, and re-layouts: none -> 8.56 us  [the longest x4 4.28 us: per_device(): lax.dynamic_update_slice_in_dim(full, going_up, (here - far) % ways * tur...]
    unnamed x12 -> x29, local copies, waits for them, and re-layouts: 1.38 us -> 9.32 us
  transfers between devices with their start and end apart: 3 -> 9, of which waited for: 3 -> 6; matrix products, arithmetic and copies ran while one was open for 0% -> 2% of each run, Pallas kernels for 0% -> 0%
where the time goes in v1:
time: 516 us; the launch traced here: 515 us
  waiting for transfers between devices  368 us (71%)
  blocking collectives  78.3 us (15%)
  matrix products  23 us (4%)
  local copies, waits for them, and re-layouts  20.7 us (4%)
  between operations  15.6 us (3%)
  other arithmetic  5.32 us (1%)
    reduce_scatter x1, waiting for transfers between devices, per_device(): lax.psum_scatter(lax.dot_general(full_head, dlogits, (((1,), (1,)), ((),...  217 us
    ppermute x4, waiting for transfers between devices, per_device(): lax.ppermute(going_up, 'seq', [(d, (d + 1) % ways) for d in range(ways)])  82.6 us
    psum x1, blocking collectives, per_device(): lax.psum((jnp.dot(queries, pooled.T, precision=highest), flops_part), 'vo...  78.3 us
    psum x1, waiting for transfers between devices, per_device(): totals = lax.psum(local_sums, 'seq')  68.6 us
  transfers between devices with their start and end apart: 9, of which 6 were waited for; matrix products, arithmetic and copies ran while one was open for 2% of the time, Pallas kernels for 0%

profile of v1, /device:TPU:2, one launch (start us, length us, event | category | flops | bytes accessed | tf_op | source)
XLA Modules:
  0.0 515.0 jit_solution(1638162825314162774)
XLA Ops:
  7.3 1.7 collective-permute-start.1
  9.0 23.9 %collective-permute-done = bf16[512,2048]{1,0:T(8,128)(2,1)S(1)} collective-permute-done((bf16[512,2048]{1,0:T(8,128)(2,1)}, bf16[512,2048]{1,0:T(8,128)(2,1)S(1)}, u32[]{:S(2)}, u32[]{:S(2)}) %collective-permute-start) | collective-permute-done | bytes 2097184 | tf_op jit(solution)/shard_map/ppermute | solution.py:46
  32.9 1.3 copy-done.3
  34.2 1.7 collective-permute-start.3
  36.0 23.7 %collective-permute-done.2 = bf16[512,2048]{1,0:T(8,128)(2,1)S(1)} collective-permute-done((bf16[512,2048]{1,0:T(8,128)(2,1)S(1)}, bf16[512,2048]{1,0:T(8,128)(2,1)S(1)}, u32[]{:S(2)}, u32[]{:S(2)}) %collective-permute-start.2) | collective-permute-done | bytes 2097184 | tf_op jit(solution)/shard_map/ppermute | solution.py:46
  61.7 23.5 %collective-permute-done.4 = bf16[512,2048]{1,0:T(8,128)(2,1)} collective-permute-done((bf16[512,2048]{1,0:T(8,128)(2,1)S(1)}, bf16[512,2048]{1,0:T(8,128)(2,1)}, u32[]{:S(2)}, u32[]{:S(2)}) %collective-permute-start.4) | collective-permute-done | bytes 2097184 | tf_op jit(solution)/shard_map/ppermute | solution.py:46
  86.8 2.0 broadcast_in_dim.3
  89.2 1.3 copy-done.4
  90.8 1.3 copy-done.6
  92.4 1.3 copy-done.8
  94.0 1.9 constant_dynamic-update-slice_fusion.3
  95.8 1.9 constant_dynamic-update-slice_fusion.2
  97.7 1.9 constant_dynamic-update-slice_fusion.1
  99.6 11.4 %collective-permute-done.6 = bf16[512,2048]{1,0:T(8,128)(2,1)} collective-permute-done((bf16[512,2048]{1,0:T(8,128)(2,1)}, bf16[512,2048]{1,0:T(8,128)(2,1)}, u32[]{:S(2)}, u32[]{:S(2)}) %collective-permute-start.6) | collective-permute-done | bytes 2097184 | tf_op jit(solution)/shard_map/ppermute | solution.py:46
  111.0 1.9 constant_dynamic-update-slice_fusion
  112.9 5.1 fusion.28
  118.7 1.3 copy-done.13
  120.0 2.2 fusion.1
  122.3 68.6 %all-reduce.3.cloned.1.call-done = f32[32,2048]{1,0:T(8,128)} async-done(((f32[32,2048]{1,0:T(8,128)}), f32[32,2048]{1,0:T(8,128)}) %all-reduce.3.cloned.1.call-update) | async-done | bytes 262160 | tf_op jit(solution)/shard_map/psum | solution.py:60
  194.5 78.3 %all-reduce = (f32[16,32]{1,0:T(8,128)S(1)}, f32[1]{0:T(128)}) all-reduce(f32[16,32]{1,0:T(8,128)S(1)} %convolution_bitcast_fusion, f32[1]{0:T(128)} %bitcast.6), channel_id=1, replica_groups=mesh['seq'=8,'vocab'=32] {'vocab'}, use_global_device_ids=true, to_apply=%region_2.3 | all-reduce | flops 513 | bytes 4104 | tf_op jit(solution)/shard_map/psum | solution.py:64
  272.9 1.4 fusion
  274.2 3.0 select_convert_fusion
  277.3 10.1 %fusion.29 = f32[4096,256]{1,0:T(8,128)} fusion(bf16[4096,2048]{1,0:T(8,128)(2,1)} %copy-done.1, bf16[256,2048]{0,1:T(8,128)(2,1)S(1)} %select_convert_fusion), kind=kOutput, calls=%fused_computation.58 | convolution fusion | flops 4294967296 | bytes 22020096 | tf_op jit(solution)/shard_map/dot_general | solution.py:76
  289.9 216.7 %reduce-scatter.2.cloned.1.call-done = f32[128,256]{1,0:T(8,128)} async-done(((f32[4096,256]{1,0:T(8,128)}), f32[128,256]{1,0:T(8,128)}) %reduce-scatter.2.cloned.1.call-update) | async-done | bytes 131088 | tf_op jit(solution)/shard_map/reduce_scatter | solution.py:75
  (54 shorter events, 12.0 us)
Async XLA Ops:
  7.2 105.8 %copy-start = (bf16[256,4096]{1,0:T(8,128)(2,1)S(1)}, bf16[256,4096]{1,0:T(8,128)(2,1)}, u32[]{:S(2)}) copy-start(bf16[256,4096]{1,0:T(8,128)(2,1)} %param.6) | copy-start | bytes 6291460
  7.2 183.7 %all-reduce.3.cloned.1.call-start = ((), (), s32[]{:S(2)}) async-start(), calls=%async_computation.1 | async-start | bytes 524288 | tf_op jit(solution)/shard_map/psum | solution.py:60
  7.2 25.7 %collective-permute-start = (bf16[512,2048]{1,0:T(8,128)(2,1)}, bf16[512,2048]{1,0:T(8,128)(2,1)S(1)}, u32[]{:S(2)}, u32[]{:S(2)}) collective-permute-start(bf16[512,2048]{1,0:T(8,128)(2,1)} %param.7), channel_id=1, source_target_pairs={{0,32},{32,64},{64,96},{96,128},{128,160},{160,192},{192,224},{224... | collective-permute-start | bytes 6291464 | tf_op jit(solution)/shard_map/ppermute | solution.py:46
  7.3 27.0 %collective-permute-start.1 = (bf16[512,2048]{1,0:T(8,128)(2,1)}, bf16[512,2048]{1,0:T(8,128)(2,1)S(1)}, u32[]{:S(2)}, u32[]{:S(2)}) collective-permute-start(bf16[512,2048]{1,0:T(8,128)(2,1)} %param.7), channel_id=1, source_target_pairs={{0,224},{32,0},{64,32},{96,64},{128,96},{160,128},{192,160},{224,1... | collective-permute-start | bytes 6291464 | tf_op jit(solution)/shard_map/ppermute | solution.py:49
  32.9 1.3 copy-start.3
  34.2 25.5 %collective-permute-start.2 = (bf16[512,2048]{1,0:T(8,128)(2,1)S(1)}, bf16[512,2048]{1,0:T(8,128)(2,1)S(1)}, u32[]{:S(2)}, u32[]{:S(2)}) collective-permute-start(bf16[512,2048]{1,0:T(8,128)(2,1)S(1)} %collective-permute-done), channel_id=1, source_target_pairs={{0,32},{32,64},{64,96},{96,128},{128,160},{160,192},{192,224},{224... | collective-permute-start | bytes 6291464 | tf_op jit(solution)/shard_map/ppermute | solution.py:46
  34.2 25.5 %copy-start.5 = (bf16[512,2048]{1,0:T(8,128)(2,1)}, bf16[512,2048]{1,0:T(8,128)(2,1)S(1)}, u32[]{:S(2)}) copy-start(bf16[512,2048]{1,0:T(8,128)(2,1)S(1)} %collective-permute-done.1) | copy-start | bytes 6291460
  34.2 25.5 %collective-permute-start.3 = (bf16[512,2048]{1,0:T(8,128)(2,1)S(1)}, bf16[512,2048]{1,0:T(8,128)(2,1)}, u32[]{:S(2)}, u32[]{:S(2)}) collective-permute-start(bf16[512,2048]{1,0:T(8,128)(2,1)S(1)} %collective-permute-done.1), channel_id=1, source_target_pairs={{0,224},{32,0},{64,32},{96,64},{128,96},{160,128},{192,160},{224,1... | collective-permute-start | bytes 6291464 | tf_op jit(solution)/shard_map/ppermute | solution.py:49
  59.7 1.3 copy-start.7
  59.7 25.6 %collective-permute-start.4 = (bf16[512,2048]{1,0:T(8,128)(2,1)S(1)}, bf16[512,2048]{1,0:T(8,128)(2,1)}, u32[]{:S(2)}, u32[]{:S(2)}) collective-permute-start(bf16[512,2048]{1,0:T(8,128)(2,1)S(1)} %collective-permute-done.2), channel_id=1, source_target_pairs={{0,32},{32,64},{64,96},{96,128},{128,160},{160,192},{192,224},{224... | collective-permute-start | bytes 6291464 | tf_op jit(solution)/shard_map/ppermute | solution.py:46
  61.0 36.7 %collective-permute-start.5 = (bf16[512,2048]{1,0:T(8,128)(2,1)}, bf16[512,2048]{1,0:T(8,128)(2,1)}, u32[]{:S(2)}, u32[]{:S(2)}) collective-permute-start(bf16[512,2048]{1,0:T(8,128)(2,1)} %collective-permute-done.3), channel_id=1, source_target_pairs={{0,224},{32,0},{64,32},{96,64},{128,96},{160,128},{192,160},{224,1... | collective-permute-start | bytes 6291464 | tf_op jit(solution)/shard_map/ppermute | solution.py:49
  85.3 25.8 %collective-permute-start.6 = (bf16[512,2048]{1,0:T(8,128)(2,1)}, bf16[512,2048]{1,0:T(8,128)(2,1)}, u32[]{:S(2)}, u32[]{:S(2)}) collective-permute-start(bf16[512,2048]{1,0:T(8,128)(2,1)} %collective-permute-done.4), channel_id=1, source_target_pairs={{0,32},{32,64},{64,96},{96,128},{128,160},{160,192},{192,224},{224... | collective-permute-start | bytes 6291464 | tf_op jit(solution)/shard_map/ppermute | solution.py:46
  86.8 2.1 copy-start.2
  88.9 1.6 copy-start.4
  90.5 1.6 copy-start.6
  92.1 1.6 copy-start.8
  112.9 5.7 %copy-start.1 = (bf16[4096,2048]{1,0:T(8,128)(2,1)}, bf16[4096,2048]{1,0:T(8,128)(2,1)S(1)}, u32[]{:S(2)}) copy-start(bf16[4096,2048]{1,0:T(8,128)(2,1)S(1)} %constant_dynamic-update-slice_fusion) | copy-start | bytes 50331652
  118.7 1.4 copy-start.13
  120.0 2.2 copy-start.11
  120.0 71.9 %copy-start.10 = (s32[2048]{0:T(1024)S(1)}, s32[2048]{0:T(1024)}, u32[]{:S(2)}) copy-start(s32[2048]{0:T(1024)} %param.11) | copy-start | bytes 24580
  120.0 73.2 %copy-start.9 = (f32[16,2048]{1,0:T(8,128)S(1)}, f32[16,2048]{1,0:T(8,128)}, u32[]{:S(2)}) copy-start(f32[16,2048]{1,0:T(8,128)} %param.8) | copy-start | bytes 393220
  120.0 152.8 %copy-start.12 = (s32[32]{0:T(128)S(1)}, s32[32]{0:T(128)}, u32[]{:S(2)}) copy-start(s32[32]{0:T(128)} %param.10) | copy-start | bytes 388
  122.2 384.4 %reduce-scatter.2.cloned.1.call-start = ((), (), s32[]{:S(2)}) async-start(), calls=%async_computation.2 | async-start | bytes 4325376 | tf_op jit(solution)/shard_map/reduce_scatter | solution.py:75
Sparse Core Ops, SparseCore 0:
  122.3 68.4 all-reduce.2
  287.5 219.0 reduce-scatter.1

commit v2 on v0

--- a/solution.py
+++ b/solution.py
@@ -43,7 +43,7 @@
     fourth = squared * squared
     powered = fourth * fourth
     local_sums = jnp.dot(member, powered, precision=highest)
-    totals = lax.psum(local_sums, "seq")
+    totals = jnp.sum(lax.all_gather(local_sums, "seq"), axis=0)
     pooled = (jnp.log(totals) - jnp.log(counts)[:, None]) / sharpness
     col_mean = jnp.sum(pooled, axis=0) / passages
     flops_part = jnp.sum(weights_df * col_mean * col_mean) / vocab_total

time: 501 us -> 464 us (0.926)
  waiting for transfers between devices: 374 us -> 338 us
    psum x1 -> x0, waiting for transfers between devices: 64.3 us -> none  [per_device(): totals = lax.psum(local_sums, 'seq')]
    all_gather x0 -> x1, waiting for transfers between devices: none -> 27.8 us  [per_device(): totals = jnp.sum(lax.all_gather(local_sums, 'seq'), axis=0)]
where the time goes in v2:
time: 464 us
  waiting for transfers between devices  338 us (73%)
  blocking collectives  78.2 us (17%)
  matrix products  24 us (5%)
  between operations  15.1 us (3%)
  other arithmetic  6.13 us (1%)
    reduce_scatter x1, waiting for transfers between devices, per_device(): lax.psum_scatter(lax.dot_general(full_head, dlogits, (((1,), (1,)), ((),...  218 us
    all_gather x1, waiting for transfers between devices, per_device(): full_head = lax.all_gather(head_weight, 'seq', axis=0, tiled=True)  91.6 us
    psum x1, blocking collectives, per_device(): lax.psum((jnp.dot(queries, pooled.T, precision=highest), flops_part), 'vo...  78.2 us
    all_gather x1, waiting for transfers between devices, per_device(): totals = jnp.sum(lax.all_gather(local_sums, 'seq'), axis=0)  27.8 us
    dot_general x1, matrix products, per_device(): lax.dot_general(full_head, dlogits, (((1,), (1,)), ((), ())), preferred_e...  10.1 us
  transfers between devices with their start and end apart: 3, of which 3 were waited for; matrix products, arithmetic and copies ran while one was open for 0% of the time, Pallas kernels for 0%

profile of v2, /device:TPU:2, one launch (start us, length us, event | category | flops | bytes accessed | tf_op | source)
XLA Modules:
  0.0 463.5 jit_solution(15726876631100479260)
XLA Ops:
  7.2 0.0 all-gather.4.cloned.1.call-start
  7.2 0.7 all-gather.4.cloned.1.call-update
  7.9 0.0 all-gather.6.cloned.1.call-start
  8.0 0.1 copy.10
  8.1 0.1 reduce-window.8
  8.1 0.1 reduce
  8.3 91.6 %all-gather.4.cloned.1.call-done = bf16[4096,2048]{1,0:T(8,128)(2,1)} async-done(((bf16[512,2048]{1,0:T(8,128)(2,1)}), bf16[4096,2048]{1,0:T(8,128)(2,1)}) %all-gather.4.cloned.1.call-update) | async-done | bytes 16777232 | tf_op jit(solution)/shard_map/all_gather | solution.py:39
  99.9 8.1 %fusion.31 = f32[256,2048]{1,0:T(8,128)S(1)} fusion(bf16[256,4096]{1,0:T(8,128)(2,1)S(1)} %copy-done, bf16[4096,2048]{1,0:T(8,128)(2,1)} %all-gather.4.cloned.1.call-done), kind=kOutput, calls=%fused_computation.51 | convolution fusion | flops 4294967296 | bytes 20971520 | tf_op jit(solution)/shard_map/dot_general | solution.py:40
  108.0 1.3 copy-done.5
  109.4 1.9 fusion.3
  111.3 0.0 reduce-scatter.2.cloned.1.call-start
  111.4 27.8 %all-gather.6.cloned.1.call-done = f32[256,2048]{1,0:T(8,128)} async-done(((f32[32,2048]{1,0:T(8,128)}), f32[256,2048]{1,0:T(8,128)}) %all-gather.6.cloned.1.call-update) | async-done | bytes 2097168 | tf_op jit(solution)/shard_map/all_gather | solution.py:46
  139.1 1.7 reduce_sum.54
  140.8 0.1 fusion.8
  141.0 0.4 convolution_bitcast_fusion.1
  141.3 0.7 fusion.17
  142.6 78.2 %all-reduce = (f32[16,32]{1,0:T(8,128)S(1)}, f32[1]{0:T(128)}) all-reduce(f32[16,32]{1,0:T(8,128)S(1)} %convolution_bitcast_fusion.1, f32[1]{0:T(128)} %bitcast.6), channel_id=1, replica_groups=mesh['seq'=8,'vocab'=32] {'vocab'}, use_global_device_ids=true, to_apply=%region_2.3 | all-reduce | flops 513 | bytes 4104 | tf_op jit(solution)/shard_map/psum | solution.py:50
  220.9 0.4 fusion.2
  221.3 3.2 fusion.1
  224.5 10.1 %convolution_bitcast_fusion = f32[4096,256]{0,1:T(8,128)} fusion(bf16[256,2048]{1,0:T(8,128)(2,1)S(1)} %fusion.1, bf16[4096,2048]{1,0:T(8,128)(2,1)} %all-gather.4.cloned.1.call-done), kind=kOutput, calls=%fused_computation | convolution fusion | flops 4294967296 | bytes 22020096 | tf_op jit(solution)/shard_map/dot_general | solution.py:62
  234.6 0.6 subtract_reduce_fusion
  235.9 1.2 pad_maximum_fusion
  237.1 218.3 %reduce-scatter.2.cloned.1.call-done = f32[128,256]{0,1:T(8,128)} async-done(((f32[4096,256]{0,1:T(8,128)}), f32[128,256]{0,1:T(8,128)}) %reduce-scatter.2.cloned.1.call-update) | async-done | bytes 131088 | tf_op jit(solution)/shard_map/reduce_scatter | solution.py:61
  455.5 1.5 convert_bitcast_fusion
  (18 shorter events, 0.1 us)
Async XLA Ops:
  7.2 92.7 %copy-start = (bf16[256,4096]{1,0:T(8,128)(2,1)S(1)}, bf16[256,4096]{1,0:T(8,128)(2,1)}, u32[]{:S(2)}) copy-start(bf16[256,4096]{1,0:T(8,128)(2,1)} %param.6) | copy-start | bytes 6291460
  7.2 0.8 copy-start.3
  7.2 92.7 %all-gather.4.cloned.1.call-start = ((), (), s32[]{:S(2)}) async-start(), calls=%async_computation.1 | async-start | bytes 18874368 | tf_op jit(solution)/shard_map/all_gather | solution.py:39
  7.9 131.2 %all-gather.6.cloned.1.call-start = ((), (), s32[]{:S(2)}) async-start(), calls=%async_computation.3 | async-start | bytes 2359296 | tf_op jit(solution)/shard_map/all_gather | solution.py:46
  108.0 1.4 copy-start.5
  111.3 29.7 %copy-start.1 = (f32[16,2048]{1,0:T(8,128)S(1)}, f32[16,2048]{1,0:T(8,128)}, u32[]{:S(2)}) copy-start(f32[16,2048]{1,0:T(8,128)} %param.8) | copy-start | bytes 393220
  111.3 30.1 %copy-start.2 = (s32[2048]{0:T(1024)S(1)}, s32[2048]{0:T(1024)}, u32[]{:S(2)}) copy-start(s32[2048]{0:T(1024)} %param.11) | copy-start | bytes 24580
  111.3 109.6 %copy-start.4 = (s32[32]{0:T(128)S(1)}, s32[32]{0:T(128)}, u32[]{:S(2)}) copy-start(s32[32]{0:T(128)} %param.10) | copy-start | bytes 388
  111.3 344.2 %reduce-scatter.2.cloned.1.call-start = ((), (), s32[]{:S(2)}) async-start(), calls=%async_computation.2 | async-start | bytes 4325376 | tf_op jit(solution)/shard_map/reduce_scatter | solution.py:61
Sparse Core Ops, SparseCore 0:
  9.9 89.9 all-gather.3
  111.4 27.6 all-gather.5
  234.8 220.6 reduce-scatter.1
